TPU v7x, 256 devices: a whole 4x4x8 slice. The times are simulated.
256 devices in a mesh: req: 32 (over x, z), mlp: 8 (over y, core).
Axes of the slice: x: 4, y: 4, z: 8, core: 2. Of those that a mesh axis runs over, the one named last changes fastest.
Arguments:
- x_pages: bfloat16 [1024, 8, 4096], P('req', None, 'mlp'), may hold values from -6 to 6
- page_owner: int32 [1024], P('req'), may hold values from 0 to 31, as said below
- request_id: int32 [8192], P('req'), may hold values from 0 to 8191, as said below
- adapter_table: int32 [8192], P('req'), may hold values from 0 to 63
- ln_gain: float32 [4096], replicated, may hold values from 0.5 to 1.5
- ln_bias: float32 [4096], replicated, may hold values from -3 to 3
- w_query: bfloat16 [4096, 2048], P('req', 'mlp'), may hold values from -0.09375 to 0.09375
- w_key: bfloat16 [4096, 2048], P('req', 'mlp'), may hold values from -0.09375 to 0.09375
- w_value: bfloat16 [4096, 2048], P('req', 'mlp'), may hold values from -0.09375 to 0.09375
- w_attn_out: bfloat16 [2048, 4096], P('mlp', 'req'), may hold values from -0.125 to 0.125
- down_query: bfloat16 [4096, 1024], P('mlp'), may hold values from -0.09375 to 0.09375
- up_query: bfloat16 [1024, 2048], P(None, 'mlp'), may hold values from -1.5 to 1.5
- down_value: bfloat16 [4096, 1024], P('mlp'), may hold values from -0.09375 to 0.09375
- up_value: bfloat16 [1024, 2048], P(None, 'mlp'), may hold values from -1.5 to 1.5
- w_fc_in: bfloat16 [4096, 8192], P('req', 'mlp'), may hold values from -0.09375 to 0.09375
- b_fc_in: float32 [8192], P('mlp'), may hold values from -3 to 3
- down_fc: bfloat16 [4096, 1024], P('mlp'), may hold values from -0.09375 to 0.09375
- up_fc: bfloat16 [1024, 8192], P(None, 'mlp'), may hold values from -1.5 to 1.5
- w_fc_out: bfloat16 [8192, 4096], P('mlp', 'req'), may hold values from -0.0625 to 0.0625
- b_fc_out: float32 [4096], P('mlp'), may hold values from -3 to 3
Outputs:
- out_pages: bfloat16 [1024, 8, 4096], P('req', None, 'mlp')
Inputs may be any that keep to these rules, and one draw needn't show every extreme that they name: `page_owner`: every owner receives exactly 32 pages, at most 2 of them from one device, and some device sends exactly 2 pages to some owner. `request_id`: ids never fall; every request lies inside one owner's block of 256 rows, and the ids of block k lie in k * 256 to k * 256 + 255; some request is 256 long.
All inputs are finite; a program needn't handle non-finite values.
Results may differ from a plain program's by a relative error of at most 0.006.
Values may be sent and summed in bfloat16 or wider, within the bound.
No kernel may reach another device: no remote copies, remote signals or barrier semaphores. Data moves between devices by JAX's collectives and lax.ppermute only.
A program may use at most 128 MiB of HBM per device.

v0:
```python
import jax
import jax.numpy as jnp
from jax import lax
from jax.sharding import PartitionSpec as P

HS = 256
ROT = 64
NAD = 64
R = 16
EPS = 1e-05


def gelu_tanh(v):
    return 0.5 * v * (1.0 + jnp.tanh(0.7978845608028654 * (v + 0.044715 * v * v * v)))


def rotate(block, pos):
    half = ROT // 2
    freq = jnp.power(10000.0, -jnp.arange(half).astype(jnp.float32) * 2.0 / ROT)
    angle = pos.astype(jnp.float32)[:, None, None] * freq[None, None, :]
    cosine = jnp.cos(angle)
    sine = jnp.sin(angle)
    even = block[:, :, 0:ROT:2]
    odd = block[:, :, 1:ROT:2]
    turned = jnp.stack([even * cosine - odd * sine, odd * cosine + even * sine], axis=-1)
    turned = turned.reshape(block.shape[0], block.shape[1], ROT)
    return jnp.concatenate([turned, block[:, :, ROT:]], axis=2)


def on_device(
    x_pages,
    page_owner,
    request_id,
    adapter_table,
    ln_gain,
    ln_bias,
    w_query,
    w_key,
    w_value,
    w_attn_out,
    down_query,
    up_query,
    down_value,
    up_value,
    w_fc_in,
    b_fc_in,
    down_fc,
    up_fc,
    w_fc_out,
    b_fc_out,
):
    groups = lax.axis_size("req")
    pg_dev = x_pages.shape[0]
    page_len = x_pages.shape[1]
    width_m = x_pages.shape[2]
    tok = request_id.shape[0]
    per_owner = pg_dev // groups + 1
    slots = groups * per_owner
    page_iota = jnp.arange(pg_dev)
    earlier = (page_owner[None, :] == page_owner[:, None]) & (
        page_iota[None, :] < page_iota[:, None]
    )
    rank = jnp.sum(earlier.astype(jnp.int32), axis=1)
    slot = page_owner * per_owner + rank
    place = (slot[None, :] == jnp.arange(slots)[:, None]).astype(jnp.bfloat16)
    flat_pages = x_pages.reshape(pg_dev, page_len * width_m)
    outgoing = jnp.dot(place, flat_pages, preferred_element_type=jnp.float32).astype(jnp.bfloat16)
    outgoing = outgoing.reshape(groups, per_owner, page_len * width_m)
    filled = jnp.sum(place, axis=1).reshape(groups, per_owner)
    arrived, marks = (
        lax.all_to_all(outgoing, "req", split_axis=0, concat_axis=0, tiled=True),
        lax.all_to_all(filled, "req", split_axis=0, concat_axis=0, tiled=True),
    )
    valid = marks.reshape(slots).astype(jnp.float32)
    position = jnp.cumsum(valid) - 1.0
    take = (
        (position[None, :] == jnp.arange(pg_dev).astype(jnp.float32)[:, None])
        & (valid[None, :] > 0.5)
    ).astype(jnp.bfloat16)
    own_x = jnp.dot(
        take, arrived.reshape(slots, page_len * width_m), preferred_element_type=jnp.float32
    )
    own_x = own_x.astype(jnp.bfloat16).reshape(tok, width_m)
    column = lax.axis_index("mlp") * width_m
    whole = lax.all_gather(own_x, "mlp", axis=1, tiled=True).astype(jnp.float32)
    mean = jnp.mean(whole, axis=1, keepdims=True)
    var = jnp.mean(jnp.square(whole - mean), axis=1, keepdims=True)
    full_ln = ((whole - mean) * lax.rsqrt(var + EPS) * ln_gain + ln_bias).astype(jnp.bfloat16)
    ln_m = lax.dynamic_slice_in_dim(full_ln, column, width_m, 1)
    local_req = request_id - lax.axis_index("req") * tok
    lookup = local_req[:, None] == jnp.arange(tok)[None, :]
    adapter = jnp.sum(jnp.where(lookup, adapter_table[None, :], 0), axis=1)
    onehot = (adapter[:, None] == jnp.arange(NAD)[None, :]).astype(jnp.float32)
    onehot_low = onehot.astype(jnp.bfloat16)

    def pick(down):
        spread = jnp.dot(ln_m, down, preferred_element_type=jnp.float32).reshape(tok, NAD, R)
        return jnp.sum(spread * onehot[:, :, None], axis=1)

    picked = lax.psum((pick(down_query), pick(down_value), pick(down_fc)), "mlp")

    def lift(chosen, up):
        expanded = (onehot_low[:, :, None] * chosen.astype(jnp.bfloat16)[:, None, :]).reshape(
            tok, NAD * R
        )
        return jnp.dot(expanded, up, preferred_element_type=jnp.float32)

    row_iota = jnp.arange(tok)
    start = jnp.sum((request_id[None, :] < request_id[:, None]).astype(jnp.int32), axis=1)
    pos = row_iota - start
    mask = (request_id[:, None] == request_id[None, :]) & (row_iota[None, :] <= row_iota[:, None])
    heads_w = w_query.shape[1]
    pieces = (
        lax.all_gather(w_query, "req", axis=0, tiled=True),
        lax.all_gather(w_key, "req", axis=0, tiled=True),
        lax.all_gather(w_value, "req", axis=0, tiled=True),
    )
    cols = full_ln
    base_q, base_k, base_v = tuple(
        [jnp.dot(cols, piece, preferred_element_type=jnp.float32) for piece in pieces]
    )
    query = rotate(
        (base_q + lift(picked[0], up_query)).reshape(tok, heads_w // HS, HS), pos
    ).astype(jnp.bfloat16)
    keys = rotate(base_k.reshape(tok, heads_w // HS, HS), pos).astype(jnp.bfloat16)
    value = (
        (base_v + lift(picked[1], up_value)).astype(jnp.bfloat16).reshape(tok, heads_w // HS, HS)
    )
    scores = jnp.einsum("qhd,khd->hqk", query, keys, preferred_element_type=jnp.float32) * HS ** (
        -0.5
    )
    scores = jnp.where(mask[None, :, :], scores, -1e30)
    top = jnp.max(scores, axis=2, keepdims=True)
    weights = jnp.exp(scores - top)
    probs = (weights / jnp.sum(weights, axis=2, keepdims=True)).astype(jnp.bfloat16)
    mixed_heads = jnp.einsum("hqk,khd->qhd", probs, value, preferred_element_type=jnp.float32)
    attn = mixed_heads.astype(jnp.bfloat16).reshape(tok, heads_w)
    cols = full_ln
    hidden_pre = jnp.dot(
        cols, lax.all_gather(w_fc_in, "req", axis=0, tiled=True), preferred_element_type=jnp.float32
    )
    hidden_pre = hidden_pre + lift(picked[2], up_fc) + b_fc_in
    hidden = gelu_tanh(hidden_pre).astype(jnp.bfloat16)
    pieces = (
        lax.all_gather(w_attn_out, "req", axis=1, tiled=True),
        lax.all_gather(w_fc_out, "req", axis=1, tiled=True),
    )
    part = jnp.dot(attn, pieces[0], preferred_element_type=jnp.float32) + jnp.dot(
        hidden, pieces[1], preferred_element_type=jnp.float32
    )
    shares = lax.psum_scatter(part, "mlp", scatter_dimension=1, tiled=True)
    result = (own_x.astype(jnp.float32) + shares + b_fc_out).astype(jnp.bfloat16)
    back_flat = result.reshape(pg_dev, page_len * width_m)
    leaving = jnp.dot(take.T, back_flat, preferred_element_type=jnp.float32).astype(jnp.bfloat16)
    leaving = leaving.reshape(groups, per_owner, page_len * width_m)
    returned = lax.all_to_all(leaving, "req", split_axis=0, concat_axis=0, tiled=True)
    pages_back = jnp.dot(
        place.T, returned.reshape(slots, page_len * width_m), preferred_element_type=jnp.float32
    )
    return pages_back.astype(jnp.bfloat16).reshape(pg_dev, page_len, width_m)


def solution(mesh):
    in_specs = (
        P("req", None, "mlp"),
        P("req"),
        P("req"),
        P("req"),
        P(),
        P(),
        P("req", "mlp"),
        P("req", "mlp"),
        P("req", "mlp"),
        P("mlp", "req"),
        P("mlp", None),
        P(None, "mlp"),
        P("mlp", None),
        P(None, "mlp"),
        P("req", "mlp"),
        P("mlp"),
        P("mlp", None),
        P(None, "mlp"),
        P("mlp", "req"),
        P("mlp"),
    )
    out_specs = P("req", None, "mlp")
    return jax.shard_map(
        on_device, mesh=mesh, in_specs=in_specs, out_specs=out_specs, check_vma=False
    )
```

profile of v0, /device:TPU:57, one launch (start us, length us, event | category | flops | bytes accessed | tf_op | source)
XLA Modules:
  0.0 669.1 jit_solution(17255531953203514862)
XLA Ops:
  6.5 1.0 convert_reduce_fusion.3
  9.0 10.6 %all-to-all-start = ((bf16[32,1,2]{2,1,0:T(2,128)(2,1)}), bf16[32,1,2]{2,1,0:T(2,128)(2,1)S(1)}, u32[]{:S(2)}, u32[]{:S(2)}) async-start(bf16[32,1,2]{2,1,0:T(2,128)(2,1)} %all_to_all.16), calls=%async_computation | async-start | bytes 32768 | tf_op jit(solution)/shard_map/all_to_all | solution.py:72
  19.7 1.0 copy.46
  21.1 1.1 reshape.339
  22.3 5.1 all-to-all-done
  27.4 4.7 all-to-all-start.1
  32.6 14.9 %all-to-all-done.1 = bf16[32,2,4096]{2,1,0:T(2,128)(2,1)S(1)} async-done(((bf16[32,2,4096]{2,1,0:T(2,128)(2,1)}), bf16[32,2,4096]{2,1,0:T(2,128)(2,1)S(1)}, u32[]{:S(2)}, u32[]{:S(2)}) %all-to-all-start.1) | async-done | bytes 524320 | tf_op jit(solution)/shard_map/all_to_all | solution.py:71
  48.1 0.8 reshape.341
  53.8 21.0 %all-gather.8.cloned.1.call-done = bf16[256,4096]{1,0:T(8,128)(2,1)} async-done(((bf16[256,512]{1,0:T(8,128)(2,1)}), bf16[256,4096]{1,0:T(8,128)(2,1)}) %all-gather.8.cloned.1.call-update) | async-done | bytes 2097168 | tf_op jit(solution)/shard_map/all_gather | solution.py:85
  74.8 2.1 convert_reduce_fusion
  77.8 1.0 fusion.5
  79.6 1.4 copy-done.5
  82.6 24.0 %all-reduce = (bf16[256,16]{0,1:T(8,128)(2,1)S(1)}, bf16[256,16]{0,1:T(8,128)(2,1)S(1)}, bf16[256,16]{0,1:T(8,128)(2,1)S(1)}) all-reduce(f32[256,16]{0,1:T(8,128)S(1)} %get-tuple-element.6, f32[256,16]{0,1:T(8,128)S(1)} %get-tuple-element.7, f32[256,16]{0,1:T(8,128)S(1)} %get-tuple-element.5), channel_id=1, replica_groups=mesh['req'=32,'mlp'=8] {'mlp'}, use_global_device_ids=true, to_apply=%region_14.15 | all-reduce | flops 12288 | bytes 73728 | tf_op jit(solution)/shard_map/psum | solution.py:100
  106.6 44.5 %all-gather.12.cloned.1.call-done = bf16[4096,256]{1,0:T(8,128)(2,1)} async-done(((bf16[128,256]{1,0:T(8,128)(2,1)}), bf16[4096,256]{1,0:T(8,128)(2,1)}) %all-gather.12.cloned.1.call-update) | async-done | bytes 2097168 | tf_op jit(solution)/shard_map/all_gather | solution.py:114
  151.1 3.2 fusion.85
  155.5 73.3 %all-gather.14.cloned.1.call-done = bf16[4096,256]{1,0:T(8,128)(2,1)} async-done(((bf16[128,256]{1,0:T(8,128)(2,1)}), bf16[4096,256]{1,0:T(8,128)(2,1)}) %all-gather.14.cloned.1.call-update) | async-done | bytes 2097168 | tf_op jit(solution)/shard_map/all_gather | solution.py:115
  228.8 3.1 convolution_bitcast_fusion
  232.0 0.8 fusion.61
  233.0 0.9 fusion.40
  234.3 72.1 %all-gather.10.cloned.1.call-done = bf16[4096,256]{1,0:T(8,128)(2,1)} async-done(((bf16[128,256]{1,0:T(8,128)(2,1)}), bf16[4096,256]{1,0:T(8,128)(2,1)}) %all-gather.10.cloned.1.call-update) | async-done | bytes 2097168 | tf_op jit(solution)/shard_map/all_gather | solution.py:116
  306.4 3.0 fusion.84
  309.8 97.4 %all-gather.18.cloned.1.call-done = bf16[4096,1024]{1,0:T(8,128)(2,1)} async-done(((bf16[128,1024]{1,0:T(8,128)(2,1)}), bf16[4096,1024]{1,0:T(8,128)(2,1)}) %all-gather.18.cloned.1.call-update) | async-done | bytes 8388624 | tf_op jit(solution)/shard_map/all_gather | solution.py:140
  407.2 7.3 %fusion.86 = f32[256,1024]{1,0:T(8,128)} fusion(bf16[256,4096]{1,0:T(8,128)(2,1)} %copy-done.1, bf16[4096,1024]{1,0:T(8,128)(2,1)} %all-gather.18.cloned.1.call-done), kind=kOutput, calls=%fused_computation.132 | convolution fusion | flops 2147483648 | bytes 11534336 | tf_op jit(solution)/shard_map/dot_general | solution.py:139
  414.5 92.1 %all-gather.20.cloned.1.call-done = bf16[1024,4096]{1,0:T(8,128)(2,1)} async-done(((bf16[1024,128]{1,0:T(8,128)(2,1)}), bf16[1024,4096]{1,0:T(8,128)(2,1)}) %all-gather.20.cloned.1.call-update) | async-done | bytes 8388624 | tf_op jit(solution)/shard_map/all_gather | solution.py:146
  506.6 8.9 %fusion.16 = f32[256,4096]{1,0:T(8,128)} fusion(bf16[1024,4096]{1,0:T(8,128)(2,1)} %all-gather.20.cloned.1.call-done, f32[256,1024]{1,0:T(8,128)} %fusion.86, bf16[256,1024]{0,1:T(8,128)(2,1)S(1)} %bitcast.65, bf16[1024,1024]{1,0:T(8,128)(2,1)S(1)} %copy-done, f32[1024]{0:T(1024)S(1)} %copy-done.12), kind=kOutput, calls=%fused_computation.33 | convolution fusion | flops 2687238144 | bytes 16257024 | tf_op jit(solution)/shard_map/dot_general | solution.py:148
  515.5 67.1 %all-gather.16.cloned.1.call-done = bf16[256,4096]{1,0:T(8,128)(2,1)} async-done(((bf16[256,128]{1,0:T(8,128)(2,1)}), bf16[256,4096]{1,0:T(8,128)(2,1)}) %all-gather.16.cloned.1.call-update) | async-done | bytes 2097168 | tf_op jit(solution)/shard_map/all_gather | solution.py:145
  582.6 5.7 convolution_add_fusion
  588.3 42.6 %reduce-scatter.2.cloned.1.call-done = f32[256,512]{1,0:T(8,128)} async-done(((f32[256,4096]{1,0:T(8,128)}), f32[256,512]{1,0:T(8,128)}) %reduce-scatter.2.cloned.1.call-update) | async-done | bytes 524304 | tf_op jit(solution)/shard_map/reduce_scatter | solution.py:151
  630.9 1.1 add_convert_fusion
  632.9 27.0 %all_to_all.20 = bf16[32,2,4096]{2,1,0:T(2,128)(2,1)} all-to-all(bf16[32,2,4096]{2,1,0:T(2,128)(2,1)S(1)} %reshape.349), channel_id=1, replica_groups=mesh['req'=32,'mlp'=8] {'req'}, dimensions={0} | all-to-all | bytes 1048576 | tf_op jit(solution)/shard_map/all_to_all | solution.py:156
  660.0 1.2 reshape.350
  661.5 0.8 copy.47
  (100 shorter events, 14.1 us)
Async XLA Ops:
  6.5 500.1 %copy-start = (bf16[1024,1024]{1,0:T(8,128)(2,1)S(1)}, bf16[1024,1024]{1,0:T(8,128)(2,1)}, u32[]{:S(2)}) copy-start(bf16[1024,1024]{1,0:T(8,128)(2,1)} %param.37) | copy-start | bytes 6291460
  8.2 23.9 %copy-start.15 = (s32[32]{0:T(128)}, s32[32]{0:T(128)S(1)}, u32[]{:S(2)}) copy-start(s32[32]{0:T(128)S(1)} %multiply_add_fusion.1) | copy-start | bytes 388
  9.0 18.3 %all-to-all-start = ((bf16[32,1,2]{2,1,0:T(2,128)(2,1)}), bf16[32,1,2]{2,1,0:T(2,128)(2,1)S(1)}, u32[]{:S(2)}, u32[]{:S(2)}) async-start(bf16[32,1,2]{2,1,0:T(2,128)(2,1)} %all_to_all.16), calls=%async_computation | async-start | bytes 32768 | tf_op jit(solution)/shard_map/all_to_all | solution.py:72
  22.3 31.2 %copy-start.13 = (s32[256]{0:T(256)S(1)}, s32[256]{0:T(256)}, u32[]{:S(2)}) copy-start(s32[256]{0:T(256)} %param.22) | copy-start | bytes 3076
  22.3 31.4 %copy-start.19 = (s32[256]{0:T(256)S(1)}, s32[256]{0:T(256)}, u32[]{:S(2)}) copy-start(s32[256]{0:T(256)} %param.23) | copy-start | bytes 3076
  27.4 20.2 %all-to-all-start.1 = ((bf16[32,2,4096]{2,1,0:T(2,128)(2,1)}), bf16[32,2,4096]{2,1,0:T(2,128)(2,1)S(1)}, u32[]{:S(2)}, u32[]{:S(2)}) async-start(bf16[32,2,4096]{2,1,0:T(2,128)(2,1)} %reshape.339), calls=%async_computation.1 | async-start | bytes 1048576 | tf_op jit(solution)/shard_map/all_to_all | solution.py:71
  32.0 42.8 %all-gather.8.cloned.1.call-start = ((), (), s32[]{:S(2)}) async-start(), calls=%async_computation.4 | async-start | bytes 2359296 | tf_op jit(solution)/shard_map/all_gather | solution.py:85
  32.1 21.5 %copy-start.17 = (f32[32]{0:T(128)}, f32[32]{0:T(128)S(1)}, u32[]{:S(2)}) copy-start(f32[32]{0:T(128)S(1)} %iota_convert_fusion) | copy-start | bytes 388
  48.9 102.2 %all-gather.12.cloned.1.call-start = ((), (), s32[]{:S(2)}) async-start(), calls=%async_computation.6 | async-start | bytes 2162688 | tf_op jit(solution)/shard_map/all_gather | solution.py:114
  49.7 179.2 %all-gather.14.cloned.1.call-start = ((), (), s32[]{:S(2)}) async-start(), calls=%async_computation.7 | async-start | bytes 2162688 | tf_op jit(solution)/shard_map/all_gather | solution.py:115
  50.4 256.0 %all-gather.10.cloned.1.call-start = ((), (), s32[]{:S(2)}) async-start(), calls=%async_computation.5 | async-start | bytes 2162688 | tf_op jit(solution)/shard_map/all_gather | solution.py:116
  51.0 356.2 %all-gather.18.cloned.1.call-start = ((), (), s32[]{:S(2)}) async-start(), calls=%async_computation.9 | async-start | bytes 8650752 | tf_op jit(solution)/shard_map/all_gather | solution.py:140
  51.6 455.1 %all-gather.20.cloned.1.call-start = ((), (), s32[]{:S(2)}) async-start(), calls=%async_computation.10 | async-start | bytes 8650752 | tf_op jit(solution)/shard_map/all_gather | solution.py:146
  52.1 530.4 %all-gather.16.cloned.1.call-start = ((), (), s32[]{:S(2)}) async-start(), calls=%async_computation.8 | async-start | bytes 2162688 | tf_op jit(solution)/shard_map/all_gather | solution.py:145
  52.9 578.0 %reduce-scatter.2.cloned.1.call-start = ((), (), s32[]{:S(2)}) async-start(), calls=%async_computation.11 | async-start | bytes 4718592 | tf_op jit(solution)/shard_map/reduce_scatter | solution.py:151
  74.8 2.2 copy-start.2
  74.8 2.9 copy-start.10
  74.8 2.9 copy-start.11
  77.8 1.2 copy-start.4
  79.0 2.6 copy-start.1
  79.0 2.0 copy-start.5
  79.0 2.6 copy-start.6
  151.1 3.3 copy-start.8
  154.8 0.7 copy-start.7
  306.4 3.0 copy-start.9
  309.8 196.8 %copy-start.12 = (f32[1024]{0:T(1024)S(1)}, f32[1024]{0:T(1024)}, u32[]{:S(2)}) copy-start(f32[1024]{0:T(1024)} %param.35) | copy-start | bytes 12292
  588.3 42.6 %copy-start.3 = (bf16[256,512]{1,0:T(8,128)(2,1)S(1)}, bf16[256,512]{1,0:T(8,128)(2,1)}, u32[]{:S(2)}) copy-start(bf16[256,512]{1,0:T(8,128)(2,1)} %reshape.341) | copy-start | bytes 786436
  588.3 42.6 %copy-start.14 = (f32[512]{0:T(512)S(1)}, f32[512]{0:T(512)}, u32[]{:S(2)}) copy-start(f32[512]{0:T(512)} %param.39) | copy-start | bytes 6148
  588.3 43.9 %copy-start.18 = (f32[32]{0:T(128)S(1)}, f32[32]{0:T(128)}, u32[]{:S(2)}) copy-start(f32[32]{0:T(128)} %copy-done.17) | copy-start | bytes 388
  632.2 29.1 %copy-start.16 = (s32[32]{0:T(128)S(1)}, s32[32]{0:T(128)}, u32[]{:S(2)}) copy-start(s32[32]{0:T(128)} %copy-done.15) | copy-start | bytes 388
Sparse Core Ops, SparseCore 0:
  49.0 25.7 all-gather.7
  77.4 73.6 all-gather.11
  153.7 75.0 all-gather.13
  231.3 75.0 all-gather.9
  308.9 98.2 all-gather.17
  409.5 97.0 all-gather.19
  509.1 73.4 all-gather.15
  588.4 42.4 reduce-scatter.1
where the time goes:
time: 670 us; the launch traced here: 669 us
  waiting for transfers between devices  534 us (80%)
  blocking collectives  51 us (8%)
  matrix products  35.3 us (5%)
  starting transfers between devices  15.6 us (2%)
  between operations  13.9 us (2%)
  local copies, waits for them, and re-layouts  10.2 us (2%)
  other arithmetic  9.33 us (1%)
    all_gather x1, waiting for transfers between devices, on_device(): lax.all_gather(w_fc_in, 'req', axis=0, tiled=True)  97.4 us
    all_gather x1, waiting for transfers between devices, on_device(): lax.all_gather(w_fc_out, 'req', axis=1, tiled=True)  92.1 us
    all_gather x1, waiting for transfers between devices, on_device(): lax.all_gather(w_key, 'req', axis=0, tiled=True)  73.3 us
    all_gather x1, waiting for transfers between devices, on_device(): lax.all_gather(w_value, 'req', axis=0, tiled=True)  72.1 us
    all_gather x1, waiting for transfers between devices, on_device(): lax.all_gather(w_attn_out, 'req', axis=1, tiled=True)  67.1 us
    all_gather x1, waiting for transfers between devices, on_device(): lax.all_gather(w_query, 'req', axis=0, tiled=True)  44.5 us
    reduce_scatter x1, waiting for transfers between devices, on_device(): shares = lax.psum_scatter(part, 'mlp', scatter_dimension=1, tiled=True)  42.6 us
    all_to_all x1, blocking collectives, on_device(): lax.all_to_all(leaving, 'req', split_axis=0, concat_axis=0, tiled=True)  27 us
  transfers between devices with their start and end apart: 10, of which 10 were waited for; matrix products, arithmetic and copies ran while one was open for 6% of the time, Pallas kernels for 0%

commit v1 on v0

--- a/solution.py
+++ b/solution.py
@@ -82,7 +82,9 @@
     )
     own_x = own_x.astype(jnp.bfloat16).reshape(tok, width_m)
     column = lax.axis_index("mlp") * width_m
-    whole = lax.all_gather(own_x, "mlp", axis=1, tiled=True).astype(jnp.float32)
+    whole = jnp.concatenate(
+        lax.all_to_all(jnp.stack([own_x] * lax.axis_size("mlp")), "mlp", 0, 0), axis=1
+    ).astype(jnp.float32)
     mean = jnp.mean(whole, axis=1, keepdims=True)
     var = jnp.mean(jnp.square(whole - mean), axis=1, keepdims=True)
     full_ln = ((whole - mean) * lax.rsqrt(var + EPS) * ln_gain + ln_bias).astype(jnp.bfloat16)

time: 670 us -> 604 us (0.901)
  waiting for transfers between devices: 534 us -> 455 us
  starting transfers between devices: 15.6 us -> 23 us
    all_gather x1, waiting for transfers between devices: 44.5 us -> 0.01 us  [on_device(): lax.all_gather(w_query, 'req', axis=0, tiled=True)]
    all_gather x1, waiting for transfers between devices: 73.3 us -> 34.8 us  [on_device(): lax.all_gather(w_key, 'req', axis=0, tiled=True)]
    all_to_all x0 -> x1, waiting for transfers between devices: none -> 23.6 us  [on_device(): lax.all_to_all(jnp.stack([own_x] * lax.axis_size('mlp')), 'mlp', 0, 0)]
    all_gather x1 -> x0, waiting for transfers between devices: 21 us -> none  [on_device(): whole = lax.all_gather(own_x, 'mlp', axis=1, tiled=True).astype(jnp.float32)]
    all_to_all x0 -> x1, starting transfers between devices: none -> 7.51 us  [on_device(): lax.all_to_all(jnp.stack([own_x] * lax.axis_size('mlp')), 'mlp', 0, 0)]
  transfers between devices with their start and end apart: 10 -> 10, of which waited for: 10 -> 9; matrix products, arithmetic and copies ran while one was open for 6% -> 8% of each run, Pallas kernels for 0% -> 0%
where the time goes in v1:
time: 604 us; the launch traced here: 603 us
  waiting for transfers between devices  455 us (75%)
  blocking collectives  51 us (8%)
  matrix products  34.9 us (6%)
  starting transfers between devices  23 us (4%)
  between operations  13.9 us (2%)
  local copies, waits for them, and re-layouts  12.5 us (2%)
  other arithmetic  12.5 us (2%)
    all_gather x1, waiting for transfers between devices, on_device(): lax.all_gather(w_fc_in, 'req', axis=0, tiled=True)  97.4 us
    all_gather x1, waiting for transfers between devices, on_device(): lax.all_gather(w_fc_out, 'req', axis=1, tiled=True)  93 us
    all_gather x1, waiting for transfers between devices, on_device(): lax.all_gather(w_value, 'req', axis=0, tiled=True)  71.6 us
    all_gather x1, waiting for transfers between devices, on_device(): lax.all_gather(w_attn_out, 'req', axis=1, tiled=True)  67.1 us
    reduce_scatter x1, waiting for transfers between devices, on_device(): shares = lax.psum_scatter(part, 'mlp', scatter_dimension=1, tiled=True)  42.6 us
    all_gather x1, waiting for transfers between devices, on_device(): lax.all_gather(w_key, 'req', axis=0, tiled=True)  34.8 us
    all_to_all x1, blocking collectives, on_device(): lax.all_to_all(leaving, 'req', split_axis=0, concat_axis=0, tiled=True)  27 us
    psum x1, blocking collectives, on_device(): lax.psum((pick(down_query), pick(down_value), pick(down_fc)), 'mlp')  23.9 us
  transfers between devices with their start and end apart: 10, of which 9 were waited for; matrix products, arithmetic and copies ran while one was open for 8% of the time, Pallas kernels for 0%

profile of v1, /device:TPU:57, one launch (start us, length us, event | category | flops | bytes accessed | tf_op | source)
XLA Modules:
  0.0 603.3 jit_solution(3950781582374520612)
XLA Ops:
  12.3 10.6 %all-to-all-start = ((bf16[32,1,2]{2,1,0:T(2,128)(2,1)}), bf16[32,1,2]{2,1,0:T(2,128)(2,1)S(1)}, u32[]{:S(2)}, u32[]{:S(2)}) async-start(bf16[32,1,2]{2,1,0:T(2,128)(2,1)} %all_to_all.20), calls=%async_computation | async-start | bytes 32768 | tf_op jit(solution)/shard_map/all_to_all | solution.py:72
  22.9 1.0 copy.49
  24.4 1.1 reshape.350
  25.5 5.1 all-to-all-done
  30.7 4.6 all-to-all-start.1
  35.9 16.4 %all-to-all-done.1 = bf16[32,2,4096]{2,1,0:T(2,128)(2,1)S(1)} async-done(((bf16[32,2,4096]{2,1,0:T(2,128)(2,1)}), bf16[32,2,4096]{2,1,0:T(2,128)(2,1)S(1)}, u32[]{:S(2)}, u32[]{:S(2)}) %all-to-all-start.1) | async-done | bytes 524320 | tf_op jit(solution)/shard_map/all_to_all | solution.py:71
  53.1 1.4 stack.27
  54.5 7.5 %all-to-all-start.2 = ((bf16[8,256,512]{1,2,0:T(8,128)(2,1)}), bf16[8,256,512]{1,2,0:T(8,128)(2,1)}, u32[]{:S(2)}, u32[]{:S(2)}) async-start(bf16[8,256,512]{1,2,0:T(8,128)(2,1)} %stack.27), calls=%async_computation.2 | async-start | bytes 4194304 | tf_op jit(solution)/shard_map/all_to_all | solution.py:86
  63.0 23.6 %all-to-all-done.2 = bf16[8,256,512]{1,2,0:T(8,128)(2,1)} async-done(((bf16[8,256,512]{1,2,0:T(8,128)(2,1)}), bf16[8,256,512]{1,2,0:T(8,128)(2,1)}, u32[]{:S(2)}, u32[]{:S(2)}) %all-to-all-start.2) | async-done | bytes 2097184 | tf_op jit(solution)/shard_map/all_to_all | solution.py:86
  86.7 2.1 convert_reduce_fusion
  88.8 2.2 multiply_reduce_fusion
  91.1 2.6 fusion.3
  94.2 1.4 copy-done.3
  97.2 23.9 %all-reduce = (bf16[256,16]{0,1:T(8,128)(2,1)S(1)}, bf16[256,16]{0,1:T(8,128)(2,1)S(1)}, bf16[256,16]{0,1:T(8,128)(2,1)S(1)}) all-reduce(f32[256,16]{0,1:T(8,128)S(1)} %get-tuple-element.6, f32[256,16]{0,1:T(8,128)S(1)} %get-tuple-element.7, f32[256,16]{0,1:T(8,128)S(1)} %get-tuple-element.5), channel_id=1, replica_groups=mesh['req'=32,'mlp'=8] {'mlp'}, use_global_device_ids=true, to_apply=%region_14.15 | all-reduce | flops 12288 | bytes 73728 | tf_op jit(solution)/shard_map/psum | solution.py:102
  121.1 0.9 broadcast_multiply_fusion.1
  122.1 3.2 fusion.83
  125.3 1.1 fusion.6
  128.1 34.8 %all-gather.11.cloned.1.call-done = bf16[4096,256]{1,0:T(8,128)(2,1)} async-done(((bf16[128,256]{1,0:T(8,128)(2,1)}), bf16[4096,256]{1,0:T(8,128)(2,1)}) %all-gather.11.cloned.1.call-update) | async-done | bytes 2097168 | tf_op jit(solution)/shard_map/all_gather | solution.py:117
  162.8 3.1 convolution_bitcast_fusion
  166.4 0.9 fusion.38
  168.9 71.6 %all-gather.7.cloned.1.call-done = bf16[4096,256]{1,0:T(8,128)(2,1)} async-done(((bf16[128,256]{1,0:T(8,128)(2,1)}), bf16[4096,256]{1,0:T(8,128)(2,1)}) %all-gather.7.cloned.1.call-update) | async-done | bytes 2097168 | tf_op jit(solution)/shard_map/all_gather | solution.py:118
  240.6 3.0 fusion.82
  243.9 97.4 %all-gather.15.cloned.1.call-done = bf16[4096,1024]{1,0:T(8,128)(2,1)} async-done(((bf16[128,1024]{1,0:T(8,128)(2,1)}), bf16[4096,1024]{1,0:T(8,128)(2,1)}) %all-gather.15.cloned.1.call-update) | async-done | bytes 8388624 | tf_op jit(solution)/shard_map/all_gather | solution.py:142
  341.3 6.4 %fusion.84 = f32[256,1024]{1,0:T(8,128)S(1)} fusion(bf16[256,4096]{0,1:T(8,128)(2,1)} %copy-done.1, bf16[4096,1024]{1,0:T(8,128)(2,1)} %all-gather.15.cloned.1.call-done), kind=kOutput, calls=%fused_computation.131 | convolution fusion | flops 2147483648 | bytes 11534336 | tf_op jit(solution)/shard_map/dot_general | solution.py:141
  347.7 93.0 %all-gather.17.cloned.1.call-done = bf16[1024,4096]{1,0:T(8,128)(2,1)} async-done(((bf16[1024,128]{1,0:T(8,128)(2,1)}), bf16[1024,4096]{1,0:T(8,128)(2,1)}) %all-gather.17.cloned.1.call-update) | async-done | bytes 8388624 | tf_op jit(solution)/shard_map/all_gather | solution.py:148
  440.8 8.7 %fusion.14 = f32[256,4096]{1,0:T(8,128)} fusion(bf16[1024,4096]{1,0:T(8,128)(2,1)} %all-gather.17.cloned.1.call-done, f32[256,1024]{1,0:T(8,128)S(1)} %fusion.84, bf16[256,1024]{0,1:T(8,128)(2,1)} %bitcast.77, bf16[1024,1024]{1,0:T(8,128)(2,1)S(1)} %copy-done, f32[1024]{0:T(1024)S(1)} %copy-done.10), kind=kOutput, calls=%fused_computation.32 | convolution fusion | flops 2687238144 | bytes 16257024 | tf_op jit(solution)/shard_map/dot_general | solution.py:150
  449.5 67.1 %all-gather.13.cloned.1.call-done = bf16[256,4096]{1,0:T(8,128)(2,1)} async-done(((bf16[256,128]{1,0:T(8,128)(2,1)}), bf16[256,4096]{1,0:T(8,128)(2,1)}) %all-gather.13.cloned.1.call-update) | async-done | bytes 2097168 | tf_op jit(solution)/shard_map/all_gather | solution.py:147
  516.6 5.8 convolution_add_fusion
  522.4 42.6 %reduce-scatter.2.cloned.1.call-done = f32[256,512]{1,0:T(8,128)} async-done(((f32[256,4096]{1,0:T(8,128)}), f32[256,512]{1,0:T(8,128)}) %reduce-scatter.2.cloned.1.call-update) | async-done | bytes 524304 | tf_op jit(solution)/shard_map/reduce_scatter | solution.py:153
  565.0 1.1 add_convert_fusion
  567.1 27.0 %all_to_all.25 = bf16[32,2,4096]{2,1,0:T(2,128)(2,1)} all-to-all(bf16[32,2,4096]{2,1,0:T(2,128)(2,1)S(1)} %reshape.360), channel_id=1, replica_groups=mesh['req'=32,'mlp'=8] {'req'}, dimensions={0} | all-to-all | bytes 1048576 | tf_op jit(solution)/shard_map/all_to_all | solution.py:158
  594.1 1.2 reshape.361
  (97 shorter events, 16.4 us)
Async XLA Ops:
  6.5 434.2 %copy-start = (bf16[1024,1024]{1,0:T(8,128)(2,1)S(1)}, bf16[1024,1024]{1,0:T(8,128)(2,1)}, u32[]{:S(2)}) copy-start(bf16[1024,1024]{1,0:T(8,128)(2,1)} %param.37) | copy-start | bytes 6291460
  6.5 115.5 %all-gather.9.cloned.1.call-start = ((), (), s32[]{:S(2)}) async-start(), calls=%async_computation.6 | async-start | bytes 2162688 | tf_op jit(solution)/shard_map/all_gather | solution.py:116
  7.3 155.6 %all-gather.11.cloned.1.call-start = ((), (), s32[]{:S(2)}) async-start(), calls=%async_computation.7 | async-start | bytes 2162688 | tf_op jit(solution)/shard_map/all_gather | solution.py:117
  8.0 232.6 %all-gather.7.cloned.1.call-start = ((), (), s32[]{:S(2)}) async-start(), calls=%async_computation.5 | async-start | bytes 2162688 | tf_op jit(solution)/shard_map/all_gather | solution.py:118
  8.7 332.6 %all-gather.15.cloned.1.call-start = ((), (), s32[]{:S(2)}) async-start(), calls=%async_computation.9 | async-start | bytes 8650752 | tf_op jit(solution)/shard_map/all_gather | solution.py:142
  9.3 431.4 %all-gather.17.cloned.1.call-start = ((), (), s32[]{:S(2)}) async-start(), calls=%async_computation.10 | async-start | bytes 8650752 | tf_op jit(solution)/shard_map/all_gather | solution.py:148
  11.5 23.9 %copy-start.13 = (s32[32]{0:T(128)}, s32[32]{0:T(128)S(1)}, u32[]{:S(2)}) copy-start(s32[32]{0:T(128)S(1)} %multiply_add_fusion.1) | copy-start | bytes 388
  12.3 18.4 %all-to-all-start = ((bf16[32,1,2]{2,1,0:T(2,128)(2,1)}), bf16[32,1,2]{2,1,0:T(2,128)(2,1)S(1)}, u32[]{:S(2)}, u32[]{:S(2)}) async-start(bf16[32,1,2]{2,1,0:T(2,128)(2,1)} %all_to_all.20), calls=%async_computation | async-start | bytes 32768 | tf_op jit(solution)/shard_map/all_to_all | solution.py:72
  30.7 21.6 %all-to-all-start.1 = ((bf16[32,2,4096]{2,1,0:T(2,128)(2,1)}), bf16[32,2,4096]{2,1,0:T(2,128)(2,1)S(1)}, u32[]{:S(2)}, u32[]{:S(2)}) async-start(bf16[32,2,4096]{2,1,0:T(2,128)(2,1)} %reshape.350), calls=%async_computation.1 | async-start | bytes 1048576 | tf_op jit(solution)/shard_map/all_to_all | solution.py:71
  35.3 17.2 %copy-start.15 = (f32[32]{0:T(128)}, f32[32]{0:T(128)S(1)}, u32[]{:S(2)}) copy-start(f32[32]{0:T(128)S(1)} %iota_convert_fusion) | copy-start | bytes 388
  54.5 8.1 %copy-start.11 = (s32[256]{0:T(256)S(1)}, s32[256]{0:T(256)}, u32[]{:S(2)}) copy-start(s32[256]{0:T(256)} %param.22) | copy-start | bytes 3076
  54.5 8.3 %copy-start.17 = (s32[256]{0:T(256)S(1)}, s32[256]{0:T(256)}, u32[]{:S(2)}) copy-start(s32[256]{0:T(256)} %param.23) | copy-start | bytes 3076
  54.5 32.1 %all-to-all-start.2 = ((bf16[8,256,512]{1,2,0:T(8,128)(2,1)}), bf16[8,256,512]{1,2,0:T(8,128)(2,1)}, u32[]{:S(2)}, u32[]{:S(2)}) async-start(bf16[8,256,512]{1,2,0:T(8,128)(2,1)} %stack.27), calls=%async_computation.2 | async-start | bytes 4194304 | tf_op jit(solution)/shard_map/all_to_all | solution.py:86
  62.0 454.5 %all-gather.13.cloned.1.call-start = ((), (), s32[]{:S(2)}) async-start(), calls=%async_computation.8 | async-start | bytes 2162688 | tf_op jit(solution)/shard_map/all_gather | solution.py:147
  62.6 502.4 %reduce-scatter.2.cloned.1.call-start = ((), (), s32[]{:S(2)}) async-start(), calls=%async_computation.11 | async-start | bytes 4718592 | tf_op jit(solution)/shard_map/reduce_scatter | solution.py:153
  63.0 28.0 %copy-start.8 = (f32[4096]{0:T(1024)S(1)}, f32[4096]{0:T(1024)}, u32[]{:S(2)}) copy-start(f32[4096]{0:T(1024)} %param.25) | copy-start | bytes 49156
  63.0 28.0 %copy-start.9 = (f32[4096]{0:T(1024)S(1)}, f32[4096]{0:T(1024)}, u32[]{:S(2)}) copy-start(f32[4096]{0:T(1024)} %param.24) | copy-start | bytes 49156
  91.0 2.6 copy-start.2
  93.6 2.6 copy-start.1
  93.6 2.0 copy-start.3
  93.7 2.5 copy-start.4
  122.1 3.2 copy-start.6
  167.6 0.7 copy-start.5
  168.9 74.6 %copy-start.7 = (bf16[1024,256]{1,0:T(8,128)(2,1)S(1)}, bf16[1024,256]{1,0:T(8,128)(2,1)}, u32[]{:S(2)}) copy-start(bf16[1024,256]{1,0:T(8,128)(2,1)} %param.33) | copy-start | bytes 1572868
  243.9 196.9 %copy-start.10 = (f32[1024]{0:T(1024)S(1)}, f32[1024]{0:T(1024)}, u32[]{:S(2)}) copy-start(f32[1024]{0:T(1024)} %param.35) | copy-start | bytes 12292
  522.4 42.6 %copy-start.12 = (f32[512]{0:T(512)S(1)}, f32[512]{0:T(512)}, u32[]{:S(2)}) copy-start(f32[512]{0:T(512)} %param.39) | copy-start | bytes 6148
  522.4 43.9 %copy-start.16 = (f32[32]{0:T(128)S(1)}, f32[32]{0:T(128)}, u32[]{:S(2)}) copy-start(f32[32]{0:T(128)} %copy-done.15) | copy-start | bytes 388
  566.3 29.1 %copy-start.14 = (s32[32]{0:T(128)S(1)}, s32[32]{0:T(128)}, u32[]{:S(2)}) copy-start(s32[32]{0:T(128)} %copy-done.13) | copy-start | bytes 388
Sparse Core Ops, SparseCore 0:
  9.9 75.4 all-gather.8
  88.0 74.7 all-gather.10
  165.4 75.0 all-gather.6
  243.0 98.2 all-gather.14
  343.7 97.0 all-gather.16
  443.1 73.4 all-gather.12
  522.6 42.4 reduce-scatter.1
